TPU v7x, 32 devices: a whole 2x2x4 slice. The times are simulated.
32 devices in a mesh: outer: 4 (over y, core), inner: 8 (over z, x).
Axes of the slice: x: 2, y: 2, z: 4, core: 2. Of those that a mesh axis runs over, the one named last changes fastest.
Arguments:
- queries: bfloat16 [4, 8, 8, 64, 512], P('outer', None, 'inner'), may hold values from -240 to 240
- keys: bfloat16 [4, 8, 8, 64, 128], P('outer', None, 'inner'), may hold values from -6 to 6
- values: bfloat16 [4, 8, 8, 64, 128], P('outer', None, 'inner'), may hold values from -6 to 6
- grad_out: bfloat16 [4, 8, 8, 64, 512], P('outer', None, 'inner'), may hold values from -6 to 6
- doc_starts: int32 [4, 8, 4], replicated, may hold values from 0 to 512, as said below
Outputs:
- attn_out: bfloat16 [4, 8, 8, 64, 512], P('outer', None, 'inner')
- query_grads: bfloat16 [4, 8, 8, 64, 512], P('outer', None, 'inner')
- key_grads: bfloat16 [4, 8, 8, 64, 128], P('outer', None, 'inner')
- value_grads: bfloat16 [4, 8, 8, 64, 128], P('outer', None, 'inner')
Inputs may be any that keep to these rules, and one draw needn't show every extreme that they name: `doc_starts`: entry [o, u, j] is an offset within unit u of segment o at which a document starts, or 512 for none. The offsets below 512 of a unit are distinct, rise with j and stand before all its 512 entries. Offset 0 starts a document in every even unit except unit 0 of segments o > 0; unit 0 of such a segment and an odd unit may continue the document of the position before them (then their first entry is not 0). The last unit of every segment continues the one before it; position 0 of the sequence starts a document.
All inputs are finite; a program needn't handle non-finite values.
Results may differ from a plain program's by a relative error of at most 0.0075.
Values may be sent and summed in bfloat16 or wider, within the bound.
No kernel may reach another device: no remote copies, remote signals or barrier semaphores. Data moves between devices by JAX's collectives and lax.ppermute only.
A program may use at most 128 MiB of HBM per device.

v0:
```python
import functools
import math

import jax
import jax.numpy as jnp
from jax import lax
from jax.experimental import pallas as pl
from jax.experimental.pallas import tpu as pltpu
from jax.sharding import PartitionSpec as P


def doc_table(doc_starts, tok_dev):
    n_outer, n_inner, n_slots = doc_starts.shape
    flat_starts = doc_starts.reshape(n_outer * n_inner, n_slots)
    start_counts = jnp.sum((flat_starts < tok_dev).astype(jnp.int32), axis=1)
    first_index = jnp.cumsum(start_counts) - start_counts
    offsets = jnp.arange(tok_dev, dtype=jnp.int32)
    inside_count = jnp.sum(
        (flat_starts[:, None, :] <= offsets[None, :, None]).astype(jnp.int32), axis=2
    )
    return (first_index[:, None] + inside_count - 1).reshape(n_outer, n_inner, tok_dev)


def attention_kernel(
    order_ref, qmeta_ref, kmeta_ref, q_ref, g_ref, k_ref, v_ref,
    o_ref, dq_ref, dkv_ref, dkt_ref, dvt_ref, *, scaling, n_heads, head_dim, slot_len
):
    step = pl.program_id(0)

    @pl.when(step == 0)
    def _():
        dkt_ref[...] = jnp.zeros_like(dkt_ref)
        dvt_ref[...] = jnp.zeros_like(dvt_ref)

    k = k_ref[...]
    v = v_ref[...]
    kt = k.T
    vt = v.T
    contract_first = (((0,), (0,)), ((), ()))
    lanes = qmeta_ref.shape[1] // 2
    allowed = (qmeta_ref[:, 0:1] == kmeta_ref[0:1, :]) & (
        kmeta_ref[1:2, :] <= qmeta_ref[:, lanes : lanes + 1]
    )
    for h in range(n_heads):
        cols = slice(h * head_dim, (h + 1) * head_dim)
        q = q_ref[:, cols]
        g = g_ref[:, cols]
        scores = jnp.dot(q, kt, preferred_element_type=jnp.float32) * scaling
        scores = jnp.where(allowed, scores, -jnp.inf)
        row_max = jnp.max(scores, axis=1, keepdims=True)
        log_total = row_max + jnp.log(
            jnp.sum(jnp.exp(scores - row_max), axis=1, keepdims=True)
        )
        probs = jnp.exp(scores - log_total)
        probs_low = probs.astype(jnp.bfloat16)
        attn = jnp.dot(probs_low, v, preferred_element_type=jnp.float32).astype(jnp.bfloat16)
        o_ref[:, cols] = attn
        inner_prod = jnp.sum(
            g.astype(jnp.float32) * attn.astype(jnp.float32), axis=1, keepdims=True
        )
        grad_probs = jnp.dot(g, vt, preferred_element_type=jnp.float32)
        score_grads = (probs * (grad_probs - inner_prod)).astype(jnp.bfloat16)
        dq_ref[:, cols] = (
            jnp.dot(score_grads, k, preferred_element_type=jnp.float32) * scaling
        ).astype(jnp.bfloat16)
        dkt_ref[...] += (
            lax.dot_general(q, score_grads, contract_first, preferred_element_type=jnp.float32)
            * scaling
        )
        dvt_ref[...] += lax.dot_general(
            g, probs_low, contract_first, preferred_element_type=jnp.float32
        )

    @pl.when(step == pl.num_programs(0) - 1)
    def _():
        n_used = dkt_ref.shape[1] // slot_len
        for r in range(n_used):
            cols = slice(r * slot_len, (r + 1) * slot_len)
            slot = order_ref[r]
            dkv_ref[slot, :, 0:head_dim] = dkt_ref[:, cols].T
            dkv_ref[slot, :, head_dim : 2 * head_dim] = dvt_ref[:, cols].T
        for r in range(n_used, dkv_ref.shape[0]):
            dkv_ref[order_ref[r]] = jnp.zeros(dkv_ref.shape[1:], dkv_ref.dtype)


def attend(rows, qmeta, ctx_all, kmeta_all, order, n_keys, n_heads):
    n_rows = rows.shape[0]
    n_slots = order.shape[0]
    slot_len = ctx_all.shape[0] // n_slots
    head_dim = ctx_all.shape[1] // 2
    width_q = n_heads * head_dim
    block_q = min(256, n_rows)
    grid = (n_rows // block_q,)
    q_spec = pl.BlockSpec((block_q, width_q), lambda i, o: (i, 0))
    g_spec = pl.BlockSpec((block_q, width_q), lambda i, o: (i, 1))
    qmeta_spec = pl.BlockSpec((block_q, qmeta.shape[1]), lambda i, o: (i, 0))
    kmeta_spec = pl.BlockSpec((2, n_keys), lambda i, o: (0, 0))
    k_spec = pl.BlockSpec((n_keys, head_dim), lambda i, o: (0, 0))
    v_spec = pl.BlockSpec((n_keys, head_dim), lambda i, o: (0, 1))
    out_spec = pl.BlockSpec((block_q, width_q), lambda i, o: (i, 0))
    grads_spec = pl.BlockSpec((n_slots, slot_len, 2 * head_dim), lambda i, o: (0, 0, 0))
    kernel = functools.partial(
        attention_kernel,
        scaling=1.0 / math.sqrt(head_dim),
        n_heads=n_heads,
        head_dim=head_dim,
        slot_len=slot_len,
    )
    return pl.pallas_call(
        kernel,
        grid_spec=pltpu.PrefetchScalarGridSpec(
            num_scalar_prefetch=1,
            grid=grid,
            in_specs=[qmeta_spec, kmeta_spec, q_spec, g_spec, k_spec, v_spec],
            out_specs=[out_spec, out_spec, grads_spec],
            scratch_shapes=[
                pltpu.VMEM((head_dim, n_keys), jnp.float32),
                pltpu.VMEM((head_dim, n_keys), jnp.float32),
            ],
        ),
        out_shape=[
            jax.ShapeDtypeStruct((n_rows, width_q), jnp.bfloat16),
            jax.ShapeDtypeStruct((n_rows, width_q), jnp.bfloat16),
            jax.ShapeDtypeStruct((n_slots, slot_len, 2 * head_dim), jnp.float32),
        ],
        compiler_params=pltpu.CompilerParams(dimension_semantics=("arbitrary",)),
    )(order, qmeta, kmeta_all, rows, rows, ctx_all, ctx_all)


def shards(queries, keys, values, grad_out, doc_starts):
    n_inner = lax.axis_size("inner")
    n_outer = lax.axis_size("outer")
    n_units = queries.shape[1]
    piece_len = queries.shape[3]
    width_q = queries.shape[4]
    head_dim = keys.shape[4]
    n_heads = width_q // head_dim
    tok_dev = piece_len * n_inner
    outer_id = lax.axis_index("outer")
    inner_id = lax.axis_index("inner")
    docs_all = doc_table(doc_starts, tok_dev)
    offsets = jnp.arange(tok_dev, dtype=jnp.int32)

    def packed_for(shift):
        def pack(q, g, k, v):
            return jnp.roll(jnp.concatenate([q, g, k, v], axis=-1), -2 * shift, axis=0)

        return pack

    packed = lax.switch(
        outer_id,
        [packed_for(o) for o in range(n_outer)],
        queries[0, :, 0],
        grad_out[0, :, 0],
        keys[0, :, 0],
        values[0, :, 0],
    )
    unit_local = (inner_id + 2 * outer_id) % n_units
    arrived = lax.all_to_all(packed, "inner", 0, 0, tiled=True).reshape(tok_dev, -1)
    kv_own = arrived[:, 2 * width_q :]

    pairs_up = [(2 * p, 2 * p + 1) for p in range(n_inner // 2)]
    kv_partner = lax.ppermute(kv_own, "inner", pairs_up)

    both = ("outer", "inner")
    last_a, last_b = n_inner - 2, n_inner - 1
    lead = [(-2 * o) % n_inner for o in range(n_outer)]
    send_a = [((o - 1) * n_inner + lead[o] + r, o * n_inner + lead[o] + r)
              for o in range(1, n_outer) for r in range(2)]
    send_b = [((o - 1) * n_inner + lead[o] + r, o * n_inner + lead[o] + 1 - r)
              for o in range(1, n_outer) for r in range(2)]
    recv_a = lax.ppermute(kv_own, both, send_a)
    recv_b = lax.ppermute(kv_own, both, send_b)
    first = unit_local == 0
    kv_prev_a = jnp.where(first, recv_a, recv_b)
    kv_prev_b = jnp.where(first, recv_b, recv_a)

    unit_id = outer_id * n_units + unit_local
    before = jnp.maximum(outer_id - 1, 0)
    has_prev = (outer_id > 0) & (unit_local < 2)
    has_partner = unit_local % 2 == 1
    query_doc = docs_all[outer_id, unit_local]
    query_pos = unit_id * tok_dev + offsets
    partner_doc = jnp.where(has_partner, docs_all[outer_id, jnp.maximum(unit_local - 1, 0)], -3)
    prev_a_doc = jnp.where(has_prev, docs_all[before, last_a], -4)
    prev_b_doc = jnp.where(has_prev, docs_all[before, last_b], -5)
    key_doc = jnp.concatenate([prev_a_doc, prev_b_doc, partner_doc, query_doc])
    key_pos = jnp.concatenate(
        [
            (before * n_units + last_a) * tok_dev + offsets,
            (before * n_units + last_b) * tok_dev + offsets,
            (unit_id - 1) * tok_dev + offsets,
            query_pos,
        ]
    )
    n_slots = 8
    slot_len = tok_dev * 4 // n_slots
    slot_kv = jnp.stack([kv_prev_a, kv_prev_b, kv_partner, kv_own]).reshape(
        n_slots, slot_len, 2 * head_dim
    )
    slot_doc = key_doc.reshape(n_slots, slot_len)
    slot_pos = key_pos.reshape(n_slots, slot_len)
    needed = (
        (jnp.min(slot_doc, axis=1) <= jnp.max(query_doc))
        & (jnp.max(slot_doc, axis=1) >= jnp.min(query_doc))
        & (jnp.min(slot_pos, axis=1) <= jnp.max(query_pos))
    )
    needed = needed | (jnp.arange(n_slots) >= n_slots - 2)
    needed_i = needed.astype(jnp.int32)
    count = jnp.sum(needed_i)
    rank = jnp.where(
        needed, jnp.cumsum(needed_i) - 1, count + jnp.cumsum(1 - needed_i) - 1
    )
    slot_ids = jnp.arange(n_slots, dtype=jnp.int32)
    order = jnp.sum(
        jnp.where(rank[None, :] == slot_ids[:, None], slot_ids[None, :], 0), axis=1
    )
    kv_sorted = slot_kv[order].reshape(n_slots * slot_len, 2 * head_dim)
    kmeta_sorted = jnp.stack([slot_doc[order].reshape(-1), slot_pos[order].reshape(-1)])
    lane_width = 128
    qmeta = jnp.concatenate(
        [
            jnp.broadcast_to(query_doc[:, None], (tok_dev, lane_width)),
            jnp.broadcast_to(query_pos[:, None], (tok_dev, lane_width)),
        ],
        axis=1,
    )

    def branch(n_used):
        def run(kv_sorted, kmeta_sorted, qmeta, order):
            return attend(
                arrived, qmeta, kv_sorted, kmeta_sorted, order, n_used * slot_len, n_heads
            )

        return run

    sizes = [2, 3, 4, 5, n_slots]
    bucket = sum((count > n).astype(jnp.int32) for n in sizes[:-1])
    attn, q_grads, kv_grads = lax.switch(
        bucket,
        [branch(n) for n in sizes],
        kv_sorted,
        kmeta_sorted,
        qmeta,
        order,
    )

    kv_grads = kv_grads.reshape(4, tok_dev, 2 * head_dim)
    pairs_down = [(b, a) for a, b in pairs_up]
    low = jnp.bfloat16
    from_partner = lax.ppermute(kv_grads[2].astype(low), "inner", pairs_down)
    back_a = [(b, a) for a, b in send_a]
    back_b = [(b, a) for a, b in send_b]
    grads_a = jnp.where(first, kv_grads[0], kv_grads[1])
    grads_b = jnp.where(first, kv_grads[1], kv_grads[0])
    from_next_a = lax.ppermute(grads_a.astype(low), both, back_a)
    from_next_b = lax.ppermute(grads_b.astype(low), both, back_b)
    kv_total = (
        kv_grads[3]
        + from_partner.astype(jnp.float32)
        + from_next_a.astype(jnp.float32)
        + from_next_b.astype(jnp.float32)
    ).astype(jnp.bfloat16)

    result = jnp.concatenate([attn, q_grads, kv_total], axis=-1).reshape(
        n_inner, piece_len, -1
    )
    returned = jnp.roll(
        lax.all_to_all(result, "inner", 0, 0, tiled=True), 2 * outer_id, axis=0
    )
    shape_q = (1, n_units, 1, piece_len, width_q)
    shape_k = (1, n_units, 1, piece_len, head_dim)
    return (
        returned[..., :width_q].reshape(shape_q),
        returned[..., width_q : 2 * width_q].reshape(shape_q),
        returned[..., 2 * width_q : 2 * width_q + head_dim].reshape(shape_k),
        returned[..., 2 * width_q + head_dim :].reshape(shape_k),
    )


def solution(mesh):
    return jax.shard_map(
        shards,
        mesh=mesh,
        in_specs=(
            P("outer", None, "inner", None, None),
            P("outer", None, "inner", None, None),
            P("outer", None, "inner", None, None),
            P("outer", None, "inner", None, None),
            P(),
        ),
        out_specs=(
            P("outer", None, "inner", None, None),
            P("outer", None, "inner", None, None),
            P("outer", None, "inner", None, None),
            P("outer", None, "inner", None, None),
        ),
        check_vma=False,
    )
```

profile of v0, /device:TPU:0, one launch (start us, length us, event | category | flops | bytes accessed | tf_op | source)
XLA Modules:
  0.0 126.6 jit_solution(8165300747616209570)
XLA Ops:
  0.6 2.5 %conditional.2 = (bf16[8,64,1280]{2,1,0:T(8,128)(2,1)}) conditional(s32[]{:T(128)} %clamp.7, (bf16[8,64,512]{2,1,0:T(8,128)(2,1)}, bf16[8,64,512]{2,1,0:T(8,128)(2,1)}, bf16[8,64,128]{2,1,0:T(8,128)(2,1)}, bf16[8,64,128]{2,1,0:T(8,128)(2,1)}) %tuple.98, (bf16[8,64,512]{2,1,0:T(8,128)(2,1)}, ...), branch_computations={%region_13.14_spmd, %region_14.15_spmd, %region_15.16_spmd, %regio... | conditional | flops 5242880 | bytes 11010140 | solution.py:150
  0.7 2.5 %pad_maximum_fusion = bf16[8,64,1280]{2,1,0:T(8,128)(2,1)} fusion(bf16[8,64,128]{2,1,0:T(8,128)(2,1)} %get-tuple-element.90, bf16[8,64,128]{2,1,0:T(8,128)(2,1)} %get-tuple-element.84, bf16[8,64,512]{2,1,0:T(8,128)(2,1)} %get-tuple-element.83, bf16[8,64,512]{2,1,0:T(8,128)(2,1)} %get-tuple-element.82), kind=kLoop, calls=%fused_computation.3 | loop fusion | flops 5242880 | bytes 2621440 | tf_op jit(solution)/shard_map/cond/branch_0_fun/concatenate | solution.py:146
  3.2 7.4 %all-to-all-start = ((bf16[8,64,1280]{2,1,0:T(8,128)(2,1)}), bf16[8,64,1280]{2,1,0:T(8,128)(2,1)S(1)}, u32[]{:S(2)}, u32[]{:S(2)}) async-start(bf16[8,64,1280]{2,1,0:T(8,128)(2,1)} %get-tuple-element.189), calls=%async_computation | async-start | bytes 2621440 | tf_op jit(solution)/shard_map/all_to_all | solution.py:159
  10.6 0.1 le.67
  10.7 0.1 convert_reduce_fusion
  10.9 0.1 reshape.293
  10.9 0.1 reduce-window.21
  11.0 0.1 reduce.3
  11.1 0.1 reshape.260
  11.2 0.1 fusion.4
  11.3 0.5 broadcast.228
  11.8 1.3 %fusion.5 = (s32[512]{0:T(512)S(1)}, s32[512]{0:T(512)S(1)}, s32[512]{0:T(512)S(1)}, s32[512]{0:T(512)S(1)}, s32[]{:T(128)}, /*index=5*/s32[]{:T(128)}, s32[1,1,512]{2,1,0:T(1,128)S(1)}) fusion(pred[]{:T(512)S(6)} %and.69, s32[4,8,512]{2,1,0:T(8,128)S(1)} %fusion.4, s32[]{:T(128)S(6)} %max.6, s32[]{:T(128)S(6)} %select_n.121, s32[]{:T(128)S(6)} %max.7, ...), kind=kLoop, calls=%fused_computation.53 | loop fusion | flops 2558 | bytes 18462 | tf_op jit(solution)/shard_map/jit(_where)/select_n | solution.py:185
  13.2 0.6 iota_add_fusion
  13.8 0.2 pad_add_fusion.3
  14.0 1.9 %fusion.12 = (s32[8,1]{0,1:T(1,128)S(1)}, pred[8]{0:T(512)(128)(4,1)S(1)}) fusion(s32[8]{0:T(128)S(1)} %get-tuple-element.168, s32[]{:T(128)} %get-tuple-element.170, s32[8]{0:T(128)S(1)} %get-tuple-element.172, s32[]{:T(128)} %get-tuple-element.163, s32[8]{0:T(128)S(1)} %get-tuple-element.173, s32[]{:T(128)} %get-tuple-element.164), kind=kLoop, calls=%fused_computation.63 | loop fusion | flops 64 | bytes 148 | tf_op jit(solution)/shard_map/convert_element_type | solution.py:209
  15.9 0.2 reduce-window.22
  16.1 0.2 reduce-window.23
  16.3 0.6 convert_reduce_fusion.2
  16.9 0.6 bitcast_select_fusion
  17.6 0.1 select_reduce_fusion
  17.7 0.6 gather_fusion.1
  18.3 0.6 gather_fusion
  18.9 23.2 %all-to-all-done = bf16[8,64,1280]{2,1,0:T(8,128)(2,1)S(1)} async-done(((bf16[8,64,1280]{2,1,0:T(8,128)(2,1)}), bf16[8,64,1280]{2,1,0:T(8,128)(2,1)S(1)}, u32[]{:S(2)}, u32[]{:S(2)}) %all-to-all-start) | async-done | bytes 1310752 | tf_op jit(solution)/shard_map/all_to_all | solution.py:159
  42.1 0.7 collective-permute-start.1
  42.8 0.7 collective-permute-start
  43.5 3.3 %collective-permute-start.2 = (bf16[512,256]{1,0:T(8,128)(2,1)S(1)}, bf16[512,256]{1,0:T(8,128)(2,1)S(1)}, u32[]{:S(2)}, u32[]{:S(2)}) collective-permute-start(bf16[512,256]{1,0:T(8,128)(2,1)S(1)} %get-tuple-element.158), channel_id=1, source_target_pairs={{0,1},{2,3},{4,5},{6,7},{8,9},{10,11},{12,13},{14,15},{16,17},{18,... | collective-permute-start | bytes 786440 | tf_op jit(solution)/shard_map/ppermute | solution.py:163
  46.9 0.1 broadcast_in_dim.50
  47.0 0.1 broadcast_in_dim.49
  49.8 0.0 collective-permute-done.1
  49.8 1.8 %collective-permute-done.2 = bf16[512,256]{1,0:T(8,128)(2,1)S(1)} collective-permute-done((bf16[512,256]{1,0:T(8,128)(2,1)S(1)}, bf16[512,256]{1,0:T(8,128)(2,1)S(1)}, u32[]{:S(2)}, u32[]{:S(2)}) %collective-permute-start.2) | collective-permute-done | bytes 262176 | tf_op jit(solution)/shard_map/ppermute | solution.py:163
  51.7 1.1 pad_maximum_fusion.5
  52.8 1.8 %gather_fusion.2 = bf16[8,256,256]{2,1,0:T(8,128)(2,1)S(1)} fusion(bf16[8,256,256]{2,1,0:T(8,128)(2,1)} %bitcast.80, s32[1024]{0:T(1024)S(1)} %pad_clamp_fusion), kind=kCustom, calls=%fused_computation.2 | custom fusion | bytes 2097184 | tf_op jit(solution)/shard_map/gather | solution.py:218
  54.6 8.8 %conditional.3 = ((bf16[512,512]{1,0:T(8,128)(2,1)S(1)}, bf16[512,512]{1,0:T(8,128)(2,1)}, f32[8,256,256]{2,1,0:T(8,128)})) conditional(s32[]{:T(128)} %clamp.6, (s32[8]{0:T(128)S(1)}, s32[512,256]{1,0:T(8,128)S(1)}, s32[2,2048]{1,0:T(2,128)S(1)}, bf16[512,1280]{1,0:T(8,128)(2,1)S(1)}, ...), branch_computations={%region_17.18_spmd, %region_18.19_spmd, %region_19.20_spmd, %regio... | conditional | bytes 8 | solution.py:239
  54.7 8.8 %branch_0_fun.1 = (bf16[512,512]{1,0:T(8,128)(2,1)S(1)}, bf16[512,512]{1,0:T(8,128)(2,1)}, f32[8,256,256]{2,1,0:T(8,128)}) custom-call(s32[8]{0:T(128)S(1)} %get-tuple-element.103.order_ref, s32[512,256]{1,0:T(8,128)S(1)} %get-tuple-element.104.qmeta_ref, s32[2,2048]{1,0:T(2,128)S(1)} %get-tuple-element.105.kmeta_ref, ...), custom_call_target="tpu_custom_call" | custom-call | tf_op jit(solution)/shard_map/cond/branch_0_fun/pallas_call | solution.py:109
  63.5 1.4 %fusion.20 = (bf16[2,256,256]{2,1,0:T(8,128)(2,1)S(1)}, bf16[2,256,256]{2,1,0:T(8,128)(2,1)S(1)}, bf16[2,256,256]{2,1,0:T(8,128)(2,1)S(1)}) fusion(f32[8,256,256]{2,1,0:T(8,128)} %get-tuple-element.137, pred[]{:T(512)S(6)} %eq.29), kind=kLoop, calls=%fused_computation.78 | loop fusion | flops 262144 | bytes 1572865 | tf_op jit(solution)/shard_map/slice | solution.py:251
  64.9 0.7 collective-permute-start.4
  65.6 1.3 %collective-permute-start.3 = (bf16[512,256]{1,0:T(8,128)(2,1)S(1)}, bf16[512,256]{1,0:T(8,128)(2,1)S(1)}, u32[]{:S(2)}, u32[]{:S(2)}) collective-permute-start(bf16[512,256]{1,0:T(8,128)(2,1)S(1)} %bitcast.90), channel_id=1, source_target_pairs={{1,0},{3,2},{5,4},{7,6},{9,8},{11,10},{13,12},{15,14},{17,16},{19,... | collective-permute-start | bytes 786440 | tf_op jit(solution)/shard_map/ppermute | solution.py:251
  66.9 0.0 copy-start.9
  66.9 0.8 collective-permute-start.5
  67.7 1.1 slice.59
  68.8 7.2 %collective-permute-done.3 = bf16[512,256]{1,0:T(8,128)(2,1)S(1)} collective-permute-done((bf16[512,256]{1,0:T(8,128)(2,1)S(1)}, bf16[512,256]{1,0:T(8,128)(2,1)S(1)}, u32[]{:S(2)}, u32[]{:S(2)}) %collective-permute-start.3) | collective-permute-done | bytes 262176 | tf_op jit(solution)/shard_map/ppermute | solution.py:251
  76.1 0.1 fusion.3
  76.2 1.1 pad_maximum_fusion.4
  77.3 16.1 %all-to-all-start.1 = ((bf16[8,64,1280]{2,1,0:T(8,128)(2,1)}), bf16[8,64,1280]{2,1,0:T(8,128)(2,1)S(1)}, u32[]{:S(2)}, u32[]{:S(2)}) async-start(bf16[8,64,1280]{2,1,0:T(8,128)(2,1)} %bitcast.22), calls=%async_computation.1 | async-start | bytes 2621440 | tf_op jit(solution)/shard_map/all_to_all | solution.py:269
  93.4 30.8 %all-to-all-done.1 = bf16[8,64,1280]{2,1,0:T(8,128)(2,1)S(1)} async-done(((bf16[8,64,1280]{2,1,0:T(8,128)(2,1)}), bf16[8,64,1280]{2,1,0:T(8,128)(2,1)S(1)}, u32[]{:S(2)}, u32[]{:S(2)}) %all-to-all-start.1) | async-done | bytes 1310752 | tf_op jit(solution)/shard_map/all_to_all | solution.py:269
  124.2 0.5 fusion
  124.7 0.8 slice_bitcast_fusion.2
  125.5 1.1 slice_bitcast_fusion
  (26 shorter events, 0.3 us)
Async XLA Ops:
  3.2 7.4 %copy-start.10 = (s32[4,8,4]{1,2,0:T(4,128)S(1)}, s32[4,8,4]{1,2,0:T(4,128)}, u32[]{:S(2)}) copy-start(s32[4,8,4]{1,2,0:T(4,128)} %param.18) | copy-start | bytes 1540
  3.2 38.9 %all-to-all-start = ((bf16[8,64,1280]{2,1,0:T(8,128)(2,1)}), bf16[8,64,1280]{2,1,0:T(8,128)(2,1)S(1)}, u32[]{:S(2)}, u32[]{:S(2)}) async-start(bf16[8,64,1280]{2,1,0:T(8,128)(2,1)} %get-tuple-element.189), calls=%async_computation | async-start | bytes 2621440 | tf_op jit(solution)/shard_map/all_to_all | solution.py:159
  42.1 7.7 %collective-permute-start.1 = (bf16[512,256]{1,0:T(8,128)(2,1)S(1)}, bf16[512,256]{1,0:T(8,128)(2,1)S(1)}, u32[]{:S(2)}, u32[]{:S(2)}) collective-permute-start(bf16[512,256]{1,0:T(8,128)(2,1)S(1)} %get-tuple-element.158), channel_id=1, source_target_pairs={{6,15},{7,14},{12,21},{13,20},{18,27},{19,26}} | collective-permute-start | bytes 786440 | tf_op jit(solution)/shard_map/ppermute | solution.py:173
  42.8 7.0 %collective-permute-start = (bf16[512,256]{1,0:T(8,128)(2,1)S(1)}, bf16[512,256]{1,0:T(8,128)(2,1)S(1)}, u32[]{:S(2)}, u32[]{:S(2)}) collective-permute-start(bf16[512,256]{1,0:T(8,128)(2,1)S(1)} %get-tuple-element.158), channel_id=1, source_target_pairs={{6,14},{7,15},{12,20},{13,21},{18,26},{19,27}} | collective-permute-start | bytes 786440 | tf_op jit(solution)/shard_map/ppermute | solution.py:172
  43.5 8.2 %collective-permute-start.2 = (bf16[512,256]{1,0:T(8,128)(2,1)S(1)}, bf16[512,256]{1,0:T(8,128)(2,1)S(1)}, u32[]{:S(2)}, u32[]{:S(2)}) collective-permute-start(bf16[512,256]{1,0:T(8,128)(2,1)S(1)} %get-tuple-element.158), channel_id=1, source_target_pairs={{0,1},{2,3},{4,5},{6,7},{8,9},{10,11},{12,13},{14,15},{16,17},{18,... | collective-permute-start | bytes 786440 | tf_op jit(solution)/shard_map/ppermute | solution.py:163
  64.9 3.9 %collective-permute-start.4 = (bf16[512,256]{1,0:T(8,128)(2,1)S(1)}, bf16[512,256]{1,0:T(8,128)(2,1)S(1)}, u32[]{:S(2)}, u32[]{:S(2)}) collective-permute-start(bf16[512,256]{1,0:T(8,128)(2,1)S(1)} %bitcast.91), channel_id=1, source_target_pairs={{14,6},{15,7},{20,12},{21,13},{26,18},{27,19}} | collective-permute-start | bytes 786440 | tf_op jit(solution)/shard_map/ppermute | solution.py:256
  65.6 10.4 %collective-permute-start.3 = (bf16[512,256]{1,0:T(8,128)(2,1)S(1)}, bf16[512,256]{1,0:T(8,128)(2,1)S(1)}, u32[]{:S(2)}, u32[]{:S(2)}) collective-permute-start(bf16[512,256]{1,0:T(8,128)(2,1)S(1)} %bitcast.90), channel_id=1, source_target_pairs={{1,0},{3,2},{5,4},{7,6},{9,8},{11,10},{13,12},{15,14},{17,16},{19,... | collective-permute-start | bytes 786440 | tf_op jit(solution)/shard_map/ppermute | solution.py:251
  66.9 9.3 %copy-start.9 = (bf16[512,512]{1,0:T(8,128)(2,1)S(1)}, bf16[512,512]{1,0:T(8,128)(2,1)}, u32[]{:S(2)}) copy-start(bf16[512,512]{1,0:T(8,128)(2,1)} %get-tuple-element.136) | copy-start | bytes 1572868
  66.9 9.1 %collective-permute-start.5 = (bf16[512,256]{1,0:T(8,128)(2,1)S(1)}, bf16[512,256]{1,0:T(8,128)(2,1)S(1)}, u32[]{:S(2)}, u32[]{:S(2)}) collective-permute-start(bf16[512,256]{1,0:T(8,128)(2,1)S(1)} %bitcast.89), channel_id=1, source_target_pairs={{15,6},{14,7},{21,12},{20,13},{27,18},{26,19}} | collective-permute-start | bytes 786440 | tf_op jit(solution)/shard_map/ppermute | solution.py:257
  77.3 46.9 %all-to-all-start.1 = ((bf16[8,64,1280]{2,1,0:T(8,128)(2,1)}), bf16[8,64,1280]{2,1,0:T(8,128)(2,1)S(1)}, u32[]{:S(2)}, u32[]{:S(2)}) async-start(bf16[8,64,1280]{2,1,0:T(8,128)(2,1)} %bitcast.22), calls=%async_computation.1 | async-start | bytes 2621440 | tf_op jit(solution)/shard_map/all_to_all | solution.py:269
where the time goes:
time: 127 us
  waiting for transfers between devices  63.1 us (50%)
  starting transfers between devices  31 us (24%)
  other arithmetic  13.1 us (10%)
  Pallas kernels  8.83 us (7%)
  local copies, waits for them, and re-layouts  7.02 us (6%)
  between operations  3.53 us (3%)
    all_to_all x1, waiting for transfers between devices, shards(): lax.all_to_all(result, 'inner', 0, 0, tiled=True)  30.8 us
    all_to_all x1, waiting for transfers between devices, shards(): lax.all_to_all(packed, 'inner', 0, 0, tiled=True).reshape(tok_dev, -1)  23.2 us
    all_to_all x1, starting transfers between devices, shards(): lax.all_to_all(result, 'inner', 0, 0, tiled=True)  16.1 us
    pallas_call x1, Pallas kernels, attend(): pl.pallas_call(kernel, grid_spec=pltpu.PrefetchScalarGridSpec(num_scalar_...  8.83 us
    all_to_all x1, starting transfers between devices, shards(): lax.all_to_all(packed, 'inner', 0, 0, tiled=True).reshape(tok_dev, -1)  7.41 us
    ppermute x1, waiting for transfers between devices, shards(): from_partner = lax.ppermute(kv_grads[2].astype(low), 'inner', pairs_down)  7.22 us
    ppermute x1, starting transfers between devices, shards(): kv_partner = lax.ppermute(kv_own, 'inner', pairs_up)  3.34 us
  transfers between devices with their start and end apart: 8, of which 4 were waited for; matrix products, arithmetic and copies ran while one was open for 8% of the time, Pallas kernels for 0%

commit v1 on v0

--- a/solution.py
+++ b/solution.py
@@ -23,7 +23,7 @@
 
 def attention_kernel(
     order_ref, qmeta_ref, kmeta_ref, q_ref, g_ref, k_ref, v_ref,
-    o_ref, dq_ref, dkv_ref, dkt_ref, dvt_ref, *, scaling, n_heads, head_dim, slot_len
+    out_ref, dkv_ref, dkt_ref, dvt_ref, *, scaling, n_heads, head_dim, slot_len
 ):
     step = pl.program_id(0)
 
@@ -54,13 +54,14 @@
         probs = jnp.exp(scores - log_total)
         probs_low = probs.astype(jnp.bfloat16)
         attn = jnp.dot(probs_low, v, preferred_element_type=jnp.float32).astype(jnp.bfloat16)
-        o_ref[:, cols] = attn
+        out_ref[:, cols] = attn
         inner_prod = jnp.sum(
             g.astype(jnp.float32) * attn.astype(jnp.float32), axis=1, keepdims=True
         )
         grad_probs = jnp.dot(g, vt, preferred_element_type=jnp.float32)
         score_grads = (probs * (grad_probs - inner_prod)).astype(jnp.bfloat16)
-        dq_ref[:, cols] = (
+        dq_cols = slice((n_heads + h) * head_dim, (n_heads + h + 1) * head_dim)
+        out_ref[:, dq_cols] = (
             jnp.dot(score_grads, k, preferred_element_type=jnp.float32) * scaling
         ).astype(jnp.bfloat16)
         dkt_ref[...] += (
@@ -97,7 +98,8 @@
     kmeta_spec = pl.BlockSpec((2, n_keys), lambda i, o: (0, 0))
     k_spec = pl.BlockSpec((n_keys, head_dim), lambda i, o: (0, 0))
     v_spec = pl.BlockSpec((n_keys, head_dim), lambda i, o: (0, 1))
-    out_spec = pl.BlockSpec((block_q, width_q), lambda i, o: (i, 0))
+    out_width = 2 * width_q + 2 * head_dim
+    out_spec = pl.BlockSpec((block_q, out_width), lambda i, o: (i, 0))
     grads_spec = pl.BlockSpec((n_slots, slot_len, 2 * head_dim), lambda i, o: (0, 0, 0))
     kernel = functools.partial(
         attention_kernel,
@@ -112,15 +114,14 @@
             num_scalar_prefetch=1,
             grid=grid,
             in_specs=[qmeta_spec, kmeta_spec, q_spec, g_spec, k_spec, v_spec],
-            out_specs=[out_spec, out_spec, grads_spec],
+            out_specs=[out_spec, grads_spec],
             scratch_shapes=[
                 pltpu.VMEM((head_dim, n_keys), jnp.float32),
                 pltpu.VMEM((head_dim, n_keys), jnp.float32),
             ],
         ),
         out_shape=[
-            jax.ShapeDtypeStruct((n_rows, width_q), jnp.bfloat16),
-            jax.ShapeDtypeStruct((n_rows, width_q), jnp.bfloat16),
+            jax.ShapeDtypeStruct((n_rows, out_width), jnp.bfloat16),
             jax.ShapeDtypeStruct((n_slots, slot_len, 2 * head_dim), jnp.float32),
         ],
         compiler_params=pltpu.CompilerParams(dimension_semantics=("arbitrary",)),
@@ -236,7 +237,7 @@
 
     sizes = [2, 3, 4, 5, n_slots]
     bucket = sum((count > n).astype(jnp.int32) for n in sizes[:-1])
-    attn, q_grads, kv_grads = lax.switch(
+    out_rows, kv_grads = lax.switch(
         bucket,
         [branch(n) for n in sizes],
         kv_sorted,
@@ -262,7 +263,7 @@
         + from_next_b.astype(jnp.float32)
     ).astype(jnp.bfloat16)
 
-    result = jnp.concatenate([attn, q_grads, kv_total], axis=-1).reshape(
+    result = out_rows.at[:, 2 * width_q :].set(kv_total).reshape(
         n_inner, piece_len, -1
     )
     returned = jnp.roll(

time: 127 us -> 123 us (0.969)
  starting transfers between devices: 31 us -> 27 us
    all_to_all x1, starting transfers between devices: 16.1 us -> 11.5 us  [shards(): lax.all_to_all(result, 'inner', 0, 0, tiled=True)]
where the time goes in v1:
time: 123 us; the launch traced here: 122 us
  waiting for transfers between devices  62.7 us (51%)
  starting transfers between devices  27 us (22%)
  other arithmetic  12.7 us (10%)
  Pallas kernels  9.79 us (8%)
  local copies, waits for them, and re-layouts  6.79 us (6%)
  between operations  3.49 us (3%)
    all_to_all x1, waiting for transfers between devices, shards(): lax.all_to_all(result, 'inner', 0, 0, tiled=True)  30.8 us
    all_to_all x1, waiting for transfers between devices, shards(): lax.all_to_all(packed, 'inner', 0, 0, tiled=True).reshape(tok_dev, -1)  23.2 us
    all_to_all x1, starting transfers between devices, shards(): lax.all_to_all(result, 'inner', 0, 0, tiled=True)  11.5 us
    pallas_call x1, Pallas kernels, attend(): pl.pallas_call(kernel, grid_spec=pltpu.PrefetchScalarGridSpec(num_scalar_...  9.79 us
    ppermute x1, waiting for transfers between devices, shards(): from_partner = lax.ppermute(kv_grads[2].astype(low), 'inner', pairs_down)  7.53 us
    all_to_all x1, starting transfers between devices, shards(): lax.all_to_all(packed, 'inner', 0, 0, tiled=True).reshape(tok_dev, -1)  7.41 us
    ppermute x1, starting transfers between devices, shards(): kv_partner = lax.ppermute(kv_own, 'inner', pairs_up)  4.02 us
    concatenate x1, other arithmetic, pack(): return jnp.roll(jnp.concatenate([q, g, k, v], axis=-1), -2 * shift, axis=0)  2.51 us
  transfers between devices with their start and end apart: 8, of which 4 were waited for; matrix products, arithmetic and copies ran while one was open for 8% of the time, Pallas kernels for 0%

profile of v1, /device:TPU:0, one launch (start us, length us, event | category | flops | bytes accessed | tf_op | source)
XLA Modules:
  0.0 122.5 jit_solution(4985831653924793314)
XLA Ops:
  0.6 2.5 %conditional.2 = (bf16[8,64,1280]{2,1,0:T(8,128)(2,1)}) conditional(s32[]{:T(128)} %clamp.7, (bf16[8,64,512]{2,1,0:T(8,128)(2,1)}, bf16[8,64,512]{2,1,0:T(8,128)(2,1)}, bf16[8,64,128]{2,1,0:T(8,128)(2,1)}, bf16[8,64,128]{2,1,0:T(8,128)(2,1)}) %tuple.134, (bf16[8,64,512]{2,1,0:T(8,128)(2,1)}, ...), branch_computations={%region_13.14_spmd, %region_14.15_spmd, %region_15.16_spmd, %regio... | conditional | flops 5242880 | bytes 11010140 | solution.py:151
  0.7 2.5 %pad_maximum_fusion = bf16[8,64,1280]{2,1,0:T(8,128)(2,1)} fusion(bf16[8,64,128]{2,1,0:T(8,128)(2,1)} %get-tuple-element.167, bf16[8,64,128]{2,1,0:T(8,128)(2,1)} %get-tuple-element.166, bf16[8,64,512]{2,1,0:T(8,128)(2,1)} %get-tuple-element.165, bf16[8,64,512]{2,1,0:T(8,128)(2,1)} %get-tuple-element.164), kind=kLoop, calls=%fused_computation.7 | loop fusion | flops 5242880 | bytes 2621440 | tf_op jit(solution)/shard_map/cond/branch_0_fun/concatenate | solution.py:147
  3.2 7.4 %all-to-all-start = ((bf16[8,64,1280]{2,1,0:T(8,128)(2,1)}), bf16[8,64,1280]{2,1,0:T(8,128)(2,1)S(1)}, u32[]{:S(2)}, u32[]{:S(2)}) async-start(bf16[8,64,1280]{2,1,0:T(8,128)(2,1)} %get-tuple-element.326), calls=%async_computation | async-start | bytes 2621440 | tf_op jit(solution)/shard_map/all_to_all | solution.py:160
  10.6 0.1 le.67
  10.7 0.1 convert_reduce_fusion
  10.9 0.1 reshape.395
  10.9 0.1 reduce-window.21
  11.0 0.1 reduce.5
  11.1 0.1 reshape.322
  11.2 0.1 fusion.4
  11.3 0.5 broadcast.269
  11.8 1.3 %fusion.5 = (s32[512]{0:T(512)S(1)}, s32[512]{0:T(512)S(1)}, s32[512]{0:T(512)S(1)}, s32[512]{0:T(512)S(1)}, s32[]{:T(128)}, /*index=5*/s32[]{:T(128)}, s32[1,1,512]{2,1,0:T(1,128)S(1)}) fusion(pred[]{:T(512)S(6)} %and.73, s32[4,8,512]{2,1,0:T(8,128)S(1)} %fusion.4, s32[]{:T(128)S(6)} %max.6, s32[]{:T(128)S(6)} %select_n.121, s32[]{:T(128)S(6)} %max.7, ...), kind=kLoop, calls=%fused_computation.61 | loop fusion | flops 2558 | bytes 18462 | tf_op jit(solution)/shard_map/jit(_where)/select_n | solution.py:186
  13.2 0.6 iota_add_fusion
  13.8 0.2 pad_add_fusion.3
  14.0 1.9 %fusion.12 = (s32[8,1]{0,1:T(1,128)S(1)}, pred[8]{0:T(512)(128)(4,1)S(1)}) fusion(s32[8]{0:T(128)S(1)} %get-tuple-element.308, s32[]{:T(128)} %get-tuple-element.312, s32[8]{0:T(128)S(1)} %get-tuple-element.314, s32[]{:T(128)} %get-tuple-element.303, s32[8]{0:T(128)S(1)} %get-tuple-element.315, s32[]{:T(128)} %get-tuple-element.304), kind=kLoop, calls=%fused_computation.71 | loop fusion | flops 64 | bytes 148 | tf_op jit(solution)/shard_map/convert_element_type | solution.py:210
  15.9 0.2 reduce-window.22
  16.1 0.2 reduce-window.23
  16.3 0.6 convert_reduce_fusion.2
  16.9 0.6 bitcast_select_fusion
  17.6 0.1 select_reduce_fusion
  17.7 0.6 gather_fusion.6
  18.3 0.6 gather_fusion.5
  18.9 23.2 %all-to-all-done = bf16[8,64,1280]{2,1,0:T(8,128)(2,1)S(1)} async-done(((bf16[8,64,1280]{2,1,0:T(8,128)(2,1)}), bf16[8,64,1280]{2,1,0:T(8,128)(2,1)S(1)}, u32[]{:S(2)}, u32[]{:S(2)}) %all-to-all-start) | async-done | bytes 1310752 | tf_op jit(solution)/shard_map/all_to_all | solution.py:160
  42.1 0.7 collective-permute-start.1
  42.8 0.7 collective-permute-start
  43.5 4.0 %collective-permute-start.2 = (bf16[512,256]{1,0:T(8,128)(2,1)S(1)}, bf16[512,256]{1,0:T(8,128)(2,1)}, u32[]{:S(2)}, u32[]{:S(2)}) collective-permute-start(bf16[512,256]{1,0:T(8,128)(2,1)S(1)} %get-tuple-element.298), channel_id=1, source_target_pairs={{0,1},{2,3},{4,5},{6,7},{8,9},{10,11},{12,13},{14,15},{16,17},{18,... | collective-permute-start | bytes 786440 | tf_op jit(solution)/shard_map/ppermute | solution.py:164
  47.5 0.1 broadcast_in_dim.50
  47.7 0.1 broadcast_in_dim.49
  50.5 0.0 collective-permute-done.1
  50.5 0.0 collective-permute-done
  50.5 1.2 collective-permute-done.2
  51.7 1.1 pad_maximum_fusion.4
  52.8 11.4 %conditional.3 = ((bf16[512,1280]{1,0:T(8,128)(2,1)}, f32[8,256,256]{2,1,0:T(8,128)})) conditional(s32[]{:T(128)} %clamp.6, (bf16[4,512,256]{2,1,0:T(8,128)(2,1)S(1)}, s32[8,1]{0,1:T(1,128)S(1)}, s32[8]{0:T(128)S(1)}, s32[512,256]{1,0:T(8,128)S(1)}, s32[2,2048]{1,0:T(2,128)S(1)}, ...), branch_computations={%region_17.18_spmd.clone, %region_18.19_spmd.clone, %region_19.20_... | conditional | flops 1024 | bytes 2101320 | solution.py:240
  52.8 1.6 %gather_fusion = bf16[8,256,256]{2,1,0:T(8,128)(2,1)} fusion(bf16[8,256,256]{2,1,0:T(8,128)(2,1)S(1)} %bitcast.82, s32[1024]{0:T(1024)S(1)} %pad_clamp_fusion), kind=kCustom, calls=%fused_computation | custom fusion | bytes 2097184 | tf_op jit(solution)/shard_map/gather | solution.py:219
  54.4 9.8 %branch_0_fun.2 = (bf16[512,1280]{1,0:T(8,128)(2,1)}, f32[8,256,256]{2,1,0:T(8,128)}) custom-call(s32[8]{0:T(128)S(1)} %get-tuple-element.228.order_ref, s32[512,256]{1,0:T(8,128)S(1)} %get-tuple-element.229.qmeta_ref, s32[2,2048]{1,0:T(2,128)S(1)} %get-tuple-element.230.kmeta_ref, bf16[512,1280]{1,0:T(8,128)(2,1)S(1)} %get-tuple-element.231.q_ref.g_ref, ...), custom_call_target="tpu_custom_call" | custom-call | tf_op jit(solution)/shard_map/cond/branch_0_fun/pallas_call | solution.py:111
  64.2 1.4 %fusion.20 = (bf16[2,256,256]{2,1,0:T(8,128)(2,1)S(1)}, bf16[2,256,256]{2,1,0:T(8,128)(2,1)S(1)}, bf16[2,256,256]{2,1,0:T(8,128)(2,1)S(1)}) fusion(f32[8,256,256]{2,1,0:T(8,128)} %get-tuple-element.227, pred[]{:T(512)S(6)} %eq.26), kind=kLoop, calls=%fused_computation.87 | loop fusion | flops 262144 | bytes 1572865 | tf_op jit(solution)/shard_map/slice | solution.py:252
  65.6 0.7 collective-permute-start.4
  66.3 1.3 %collective-permute-start.3 = (bf16[512,256]{1,0:T(8,128)(2,1)S(1)}, bf16[512,256]{1,0:T(8,128)(2,1)S(1)}, u32[]{:S(2)}, u32[]{:S(2)}) collective-permute-start(bf16[512,256]{1,0:T(8,128)(2,1)S(1)} %bitcast.114), channel_id=1, source_target_pairs={{1,0},{3,2},{5,4},{7,6},{9,8},{11,10},{13,12},{15,14},{17,16},{19,... | collective-permute-start | bytes 786440 | tf_op jit(solution)/shard_map/ppermute | solution.py:252
  67.6 0.7 collective-permute-start.5
  68.3 1.1 slice.81
  69.4 0.0 collective-permute-done.4
  69.4 7.5 %collective-permute-done.3 = bf16[512,256]{1,0:T(8,128)(2,1)S(1)} collective-permute-done((bf16[512,256]{1,0:T(8,128)(2,1)S(1)}, bf16[512,256]{1,0:T(8,128)(2,1)S(1)}, u32[]{:S(2)}, u32[]{:S(2)}) %collective-permute-start.3) | collective-permute-done | bytes 262176 | tf_op jit(solution)/shard_map/ppermute | solution.py:252
  76.9 0.9 constant_dynamic-update-slice_fusion.12
  77.8 11.5 %all-to-all-start.1 = ((bf16[8,64,1280]{2,1,0:T(8,128)(2,1)}), bf16[8,64,1280]{2,1,0:T(8,128)(2,1)S(1)}, u32[]{:S(2)}, u32[]{:S(2)}) async-start(bf16[8,64,1280]{2,1,0:T(8,128)(2,1)} %bitcast.20), calls=%async_computation.1 | async-start | bytes 2621440 | tf_op jit(solution)/shard_map/all_to_all | solution.py:270
  89.3 30.8 %all-to-all-done.1 = bf16[8,64,1280]{2,1,0:T(8,128)(2,1)S(1)} async-done(((bf16[8,64,1280]{2,1,0:T(8,128)(2,1)}), bf16[8,64,1280]{2,1,0:T(8,128)(2,1)S(1)}, u32[]{:S(2)}, u32[]{:S(2)}) %all-to-all-start.1) | async-done | bytes 1310752 | tf_op jit(solution)/shard_map/all_to_all | solution.py:270
  120.2 0.5 fusion
  120.6 0.8 slice_bitcast_fusion.2
  121.4 1.1 slice_bitcast_fusion
  (24 shorter events, 0.3 us)
Async XLA Ops:
  3.2 7.4 %copy-start.9 = (s32[4,8,4]{1,2,0:T(4,128)S(1)}, s32[4,8,4]{1,2,0:T(4,128)}, u32[]{:S(2)}) copy-start(s32[4,8,4]{1,2,0:T(4,128)} %param.20) | copy-start | bytes 1540
  3.2 38.9 %all-to-all-start = ((bf16[8,64,1280]{2,1,0:T(8,128)(2,1)}), bf16[8,64,1280]{2,1,0:T(8,128)(2,1)S(1)}, u32[]{:S(2)}, u32[]{:S(2)}) async-start(bf16[8,64,1280]{2,1,0:T(8,128)(2,1)} %get-tuple-element.326), calls=%async_computation | async-start | bytes 2621440 | tf_op jit(solution)/shard_map/all_to_all | solution.py:160
  42.1 8.3 %collective-permute-start.1 = (bf16[512,256]{1,0:T(8,128)(2,1)S(1)}, bf16[512,256]{1,0:T(8,128)(2,1)S(1)}, u32[]{:S(2)}, u32[]{:S(2)}) collective-permute-start(bf16[512,256]{1,0:T(8,128)(2,1)S(1)} %get-tuple-element.298), channel_id=1, source_target_pairs={{6,15},{7,14},{12,21},{13,20},{18,27},{19,26}} | collective-permute-start | bytes 786440 | tf_op jit(solution)/shard_map/ppermute | solution.py:174
  42.8 7.7 %collective-permute-start = (bf16[512,256]{1,0:T(8,128)(2,1)S(1)}, bf16[512,256]{1,0:T(8,128)(2,1)S(1)}, u32[]{:S(2)}, u32[]{:S(2)}) collective-permute-start(bf16[512,256]{1,0:T(8,128)(2,1)S(1)} %get-tuple-element.298), channel_id=1, source_target_pairs={{6,14},{7,15},{12,20},{13,21},{18,26},{19,27}} | collective-permute-start | bytes 786440 | tf_op jit(solution)/shard_map/ppermute | solution.py:173
  43.5 8.2 %collective-permute-start.2 = (bf16[512,256]{1,0:T(8,128)(2,1)S(1)}, bf16[512,256]{1,0:T(8,128)(2,1)}, u32[]{:S(2)}, u32[]{:S(2)}) collective-permute-start(bf16[512,256]{1,0:T(8,128)(2,1)S(1)} %get-tuple-element.298), channel_id=1, source_target_pairs={{0,1},{2,3},{4,5},{6,7},{8,9},{10,11},{12,13},{14,15},{16,17},{18,... | collective-permute-start | bytes 786440 | tf_op jit(solution)/shard_map/ppermute | solution.py:164
  65.6 3.8 %collective-permute-start.4 = (bf16[512,256]{1,0:T(8,128)(2,1)S(1)}, bf16[512,256]{1,0:T(8,128)(2,1)S(1)}, u32[]{:S(2)}, u32[]{:S(2)}) collective-permute-start(bf16[512,256]{1,0:T(8,128)(2,1)S(1)} %bitcast.115), channel_id=1, source_target_pairs={{14,6},{15,7},{20,12},{21,13},{26,18},{27,19}} | collective-permute-start | bytes 786440 | tf_op jit(solution)/shard_map/ppermute | solution.py:257
  66.3 10.6 %collective-permute-start.3 = (bf16[512,256]{1,0:T(8,128)(2,1)S(1)}, bf16[512,256]{1,0:T(8,128)(2,1)S(1)}, u32[]{:S(2)}, u32[]{:S(2)}) collective-permute-start(bf16[512,256]{1,0:T(8,128)(2,1)S(1)} %bitcast.114), channel_id=1, source_target_pairs={{1,0},{3,2},{5,4},{7,6},{9,8},{11,10},{13,12},{15,14},{17,16},{19,... | collective-permute-start | bytes 786440 | tf_op jit(solution)/shard_map/ppermute | solution.py:252
  67.6 9.3 %collective-permute-start.5 = (bf16[512,256]{1,0:T(8,128)(2,1)S(1)}, bf16[512,256]{1,0:T(8,128)(2,1)S(1)}, u32[]{:S(2)}, u32[]{:S(2)}) collective-permute-start(bf16[512,256]{1,0:T(8,128)(2,1)S(1)} %bitcast.113), channel_id=1, source_target_pairs={{15,6},{14,7},{21,12},{20,13},{27,18},{26,19}} | collective-permute-start | bytes 786440 | tf_op jit(solution)/shard_map/ppermute | solution.py:258
  77.8 42.3 %all-to-all-start.1 = ((bf16[8,64,1280]{2,1,0:T(8,128)(2,1)}), bf16[8,64,1280]{2,1,0:T(8,128)(2,1)S(1)}, u32[]{:S(2)}, u32[]{:S(2)}) async-start(bf16[8,64,1280]{2,1,0:T(8,128)(2,1)} %bitcast.20), calls=%async_computation.1 | async-start | bytes 2621440 | tf_op jit(solution)/shard_map/all_to_all | solution.py:270
